TPU v7x, 512 devices: a whole 4x8x8 slice. The times are simulated.
512 devices in a mesh: req: 64 (over z, x, core), tp: 8 (over y).
Axes of the slice: x: 4, y: 8, z: 8, core: 2. Of those that a mesh axis runs over, the one named last changes fastest.
Arguments:
- queries: bfloat16 [1024, 2048], P('req', 'tp'), may hold values from -27 to 27
- fresh_cache: bfloat16 [1024, 2, 2048], P('req', None, 'tp'), may hold values from -4 to 4
- tail_cache: bfloat16 [1024, 32, 2, 2048], P('req', None, None, 'tp'), may hold values from -4 to 4
- tail_len: int32 [1024], P('req'), may hold values from 1 to 32, as said below
- pool_cache: bfloat16 [2048, 64, 2, 2048], P('req', None, None, 'tp'), may hold values from -4 to 4
- page_group: int32 [2048], P('req'), may hold values from 0 to 63, as said below
- page_start: int32 [2048], P('req'), may hold values from 0 to 16320, as said below
- prompt_len: int32 [64], replicated, may hold values from 1 to 16384, as said below
- residual: bfloat16 [1024, 2048], P('req'), may hold values from -80 to 80
- out_weight: bfloat16 [2048, 2048], P('tp'), may hold values from -0.125 to 0.125
- out_bias: bfloat16 [2048], replicated, may hold values from -0.796875 to 0.796875
- norm_gain: bfloat16 [2048], P('tp'), may hold values from 0.5 to 1.5
- norm_shift: bfloat16 [2048], P('tp'), may hold values from -0.796875 to 0.796875
Outputs:
- attention_out: bfloat16 [1024, 2048], P('req', 'tp')
- normed: bfloat16 [1024, 2048], P('req', 'tp')
Inputs may be any that keep to these rules, and one draw needn't show every extreme that they name: page_group[p] is the group whose prompt page p holds; every page holds some group's prompt; every group holds at least one page and at most 256 pages, and some group holds exactly 256; the pages of a group of n pages lie on min(n, 64) different indices of req, none holding more than ceil(n / 64) of them. The pages of a group of n pages have page_start 0, 64, ..., (n - 1) * 64, each once. `prompt_len`: a group of n pages has a prompt of (n - 1) * 64 + 1 to n * 64 positions. `tail_len`: some request has exactly 32 tail positions.
All inputs are finite; a program needn't handle non-finite values.
Results may differ from a plain program's by a relative error of at most 0.02.
Values may be sent and summed in bfloat16 or wider, within the bound.
No kernel may reach another device: no remote copies, remote signals or barrier semaphores. Data moves between devices by JAX's collectives and lax.ppermute only.
A program may use at most 64 MiB of HBM per device.

v0:
```python
import math
import jax
import jax.numpy as jnp
from jax import lax
from jax.sharding import PartitionSpec as P

HEADS = 16
HEAD = 128
PAGE = 64
masked_score = -1e30
norm_epsilon = 1e-05


def split_halves(values):
    upper_part = lax.optimization_barrier(values.astype(jnp.bfloat16))
    lower_part = (values - upper_part.astype(jnp.float32)).astype(jnp.bfloat16)
    return (upper_part, lower_part)


def local(
    queries,
    fresh_cache,
    tail_cache,
    tail_len,
    pool_cache,
    page_group,
    page_start,
    prompt_len,
    residual,
    out_weight,
    out_bias,
    norm_gain,
    norm_shift,
):
    f32 = jnp.float32
    highest = lax.Precision.HIGHEST
    row_count, feat_width = queries.shape
    heads_here = feat_width // HEAD
    inv_root = 1.0 / math.sqrt(HEAD)
    head_ids = lax.axis_index("tp") * heads_here + jnp.arange(heads_here)
    slopes = jnp.exp2(-8.0 * (head_ids.astype(f32) + 1.0) / HEADS)
    group_count = prompt_len.shape[0]
    page_count = pool_cache.shape[0]
    tail_slots = tail_cache.shape[1]
    n_req = lax.axis_size("req")
    assert group_count == n_req
    everyone = lax.all_gather(queries, "req", axis=0, tiled=True)
    by_group = everyone.reshape(group_count, row_count, heads_here, HEAD)
    safe_group = jnp.clip(page_group, 0, group_count - 1)
    page_queries = by_group[safe_group]
    page_keys = pool_cache[:, :, 0].reshape(page_count, PAGE, heads_here, HEAD)
    page_values = pool_cache[:, :, 1].reshape(page_count, PAGE, heads_here, HEAD)
    prompt_here = prompt_len[safe_group]
    positions = page_start[:, None] + jnp.arange(PAGE)[None, :]
    usable = (positions < prompt_here[:, None]) & (page_group[:, None] >= 0)
    offsets = (positions - prompt_here[:, None]).astype(f32)
    scores = (
        jnp.einsum("pqhd,pshd->pqhs", page_queries, page_keys, preferred_element_type=f32)
        * inv_root
    )
    scores = scores + slopes[None, None, :, None] * offsets[:, None, None, :]
    scores = jnp.where(usable[:, None, None, :], scores, masked_score)
    member = (page_group[:, None] == jnp.arange(group_count)[None, :]) & (page_group[:, None] >= 0)
    page_top = scores.max(-1)
    local_top = jnp.where(member[:, :, None, None], page_top[:, None], masked_score).max(0)
    page_ref = local_top[safe_group]
    weights = jnp.where(usable[:, None, None, :], jnp.exp(scores - page_ref[..., None]), 0.0)
    page_totals = weights.sum(-1)
    upper_part, lower_part = split_halves(weights)
    page_accum = jnp.einsum("pqhs,pshd->pqhd", upper_part, page_values, preferred_element_type=f32)
    page_accum = page_accum + jnp.einsum(
        "pqhs,pshd->pqhd", lower_part, page_values, preferred_element_type=f32
    )
    accum_upper, accum_lower = split_halves(page_accum.reshape(page_count, -1))
    spread = member.T.astype(jnp.bfloat16)
    group_accum = jnp.dot(spread, accum_upper, preferred_element_type=f32)
    group_accum = group_accum + jnp.dot(spread, accum_lower, preferred_element_type=f32)
    group_totals = jnp.dot(
        member.T.astype(f32), page_totals.reshape(page_count, -1), precision=highest
    )
    stats_width = row_count * heads_here
    pad_width = -(group_accum.shape[1] + 2 * stats_width) % 128
    packed = jnp.concatenate(
        [
            group_accum,
            local_top.reshape(group_count, stats_width),
            group_totals,
            jnp.zeros((group_count, pad_width), f32),
        ],
        axis=1,
    )
    arrived = lax.all_to_all(packed, "req", 0, 0, tiled=True)
    accum_width = row_count * feat_width
    part_accum = arrived[:, :accum_width].reshape(n_req, row_count, heads_here, HEAD)
    part_top = arrived[:, accum_width : accum_width + stats_width].reshape(
        n_req, row_count, heads_here
    )
    part_totals = arrived[:, accum_width + stats_width : accum_width + 2 * stats_width].reshape(
        n_req, row_count, heads_here
    )
    home_queries = queries.reshape(row_count, heads_here, HEAD)
    tail_keys = tail_cache[:, :, 0].reshape(row_count, tail_slots, heads_here, HEAD)
    tail_values = tail_cache[:, :, 1].reshape(row_count, tail_slots, heads_here, HEAD)
    fresh_keys = fresh_cache[:, 0].reshape(row_count, heads_here, HEAD)
    fresh_values = fresh_cache[:, 1].reshape(row_count, heads_here, HEAD)
    slot_ids = jnp.arange(tail_slots)
    tail_scores = (
        jnp.einsum("qhd,qjhd->qhj", home_queries, tail_keys, preferred_element_type=f32) * inv_root
    )
    tail_scores = tail_scores + slopes[None, :, None] * slot_ids.astype(f32)[None, None, :]
    tail_scores = jnp.where(
        slot_ids[None, None, :] < tail_len[:, None, None], tail_scores, masked_score
    )
    own_scores = (
        jnp.einsum("qhd,qhd->qh", home_queries, fresh_keys, preferred_element_type=f32) * inv_root
    )
    own_scores = own_scores + slopes[None, :] * tail_len.astype(f32)[:, None]
    home_top = jnp.maximum(tail_scores.max(-1), own_scores)
    row_top = jnp.maximum(home_top, part_top.max(0))
    part_scale = jnp.exp(part_top - row_top[None])
    pool_totals = jnp.sum(part_scale * part_totals, 0)
    pool_accum = jnp.sum(part_scale[..., None] * part_accum, 0)
    tail_weights = jnp.exp(tail_scores - row_top[:, :, None])
    own_weights = jnp.exp(own_scores - row_top)
    totals = tail_weights.sum(-1) + own_weights
    upper_part, lower_part = split_halves(tail_weights)
    accum = jnp.einsum("qhj,qjhd->qhd", upper_part, tail_values, preferred_element_type=f32)
    accum = accum + jnp.einsum("qhj,qjhd->qhd", lower_part, tail_values, preferred_element_type=f32)
    home_accum = accum + own_weights[:, :, None] * fresh_values.astype(f32)
    attention = ((pool_accum + home_accum) / (pool_totals + totals)[:, :, None]).astype(
        jnp.bfloat16
    )
    attention = attention.reshape(row_count, feat_width)
    partial_value = jnp.dot(attention, out_weight, preferred_element_type=f32)
    model_width = residual.shape[1]
    own_start = lax.axis_index("tp") * feat_width
    summed = lax.psum_scatter(
        partial_value.astype(jnp.bfloat16), "tp", scatter_dimension=1, tiled=True
    ).astype(jnp.float32)
    bias_mine = lax.dynamic_slice_in_dim(out_bias, own_start, feat_width, 0).astype(f32)
    attention_mine = (summed + bias_mine[None, :]).astype(jnp.bfloat16)
    residual_mine = lax.dynamic_slice_in_dim(residual, own_start, feat_width, 1).astype(f32)
    hidden_mine = residual_mine + attention_mine.astype(f32)
    first_sum, second_sum = lax.psum(
        (jnp.sum(hidden_mine, -1), jnp.sum(hidden_mine * hidden_mine, -1)), "tp"
    )
    row_mean = (first_sum / model_width)[:, None]
    mean_square = (second_sum / model_width)[:, None]
    row_var = mean_square - row_mean * row_mean
    normed = (
        (hidden_mine - row_mean)
        * lax.rsqrt(row_var + norm_epsilon)
        * norm_gain.astype(f32)[None, :]
    )
    normed = normed + norm_shift.astype(f32)[None, :]
    return (attention_mine, normed.astype(jnp.bfloat16))


def solution(mesh):
    in_specs = (
        P("req", "tp"),
        P("req", None, "tp"),
        P("req", None, None, "tp"),
        P("req"),
        P("req", None, None, "tp"),
        P("req"),
        P("req"),
        P(),
        P("req", None),
        P("tp", None),
        P(),
        P("tp"),
        P("tp"),
    )
    out_specs = (P("req", "tp"), P("req", "tp"))
    return jax.shard_map(local, mesh=mesh, in_specs=in_specs, out_specs=out_specs, check_vma=False)
```

profile of v0, /device:TPU:2, one launch (start us, length us, event | category | flops | bytes accessed | tf_op | source)
XLA Modules:
  0.0 193.3 jit_solution(1942544731091071462)
XLA Ops:
  7.2 0.7 compare_select_fusion
  7.9 0.7 broadcast_compare_fusion
  8.6 1.4 gather_fusion
  10.0 0.7 subtract_convert_fusion.5
  10.7 0.8 fusion.33
  11.5 56.0 %all_gather.3 = bf16[1024,256]{1,0:T(8,128)(2,1)S(1)} all-gather(bf16[16,256]{1,0:T(8,128)(2,1)} %param.13), channel_id=1, replica_groups=mesh['req'=64,'tp'=8] {'req'}, dimensions={0}, use_global_device_ids=true | all-gather | bytes 532480 | tf_op jit(solution)/shard_map/all_gather | solution.py:47
  67.7 0.6 gather_fusion.1
  68.3 10.7 %slice_reduce_fusion = (bf16[32,64,256]{2,1,0:T(8,128)(2,1)S(1)}, bf16[32,64,256]{2,1,0:T(8,128)(2,1)S(1)}) fusion(bf16[32,64,2,256]{3,2,1,0:T(2,128)(2,1)} %param.17), kind=kLoop, calls=%fused_computation.7 | loop fusion | bytes 4194304 | tf_op jit(solution)/shard_map/slice | solution.py:52
  79.1 0.8 fusion.50
  80.2 0.6 gather_fusion.2
  80.8 0.4 fusion.12
  81.6 0.5 fusion.1
  84.5 2.1 %copy.57 = f32[64,1,4224]{2,1,0:T(1,128)} copy(f32[64,1,4224]{2,0,1:T(8,128)S(1)} %bitcast.87) | data formatting | bytes 2162688 | tf_op jit(solution)/shard_map/all_to_all | solution.py:92
  86.6 6.3 %all-to-all-start = ((f32[64,1,4224]{2,1,0:T(1,128)}), f32[64,1,4224]{2,1,0:T(1,128)}, u32[]{:S(2)}, u32[]{:S(2)}) async-start(f32[64,1,4224]{2,1,0:T(1,128)} %copy.57), calls=%async_computation | async-start | bytes 2162688 | tf_op jit(solution)/shard_map/all_to_all | solution.py:92
  93.7 2.2 %slice_reduce_fusion.2 = (bf16[16,32,256]{2,1,0:T(8,128)(2,1)S(1)}, bf16[16,32,256]{2,1,0:T(8,128)(2,1)S(1)}) fusion(bf16[16,32,2,256]{3,2,1,0:T(2,128)(2,1)S(1)} %copy-done.1), kind=kLoop, calls=%fused_computation.22 | loop fusion | bytes 1048576 | tf_op jit(solution)/shard_map/slice | solution.py:103
  96.2 26.2 %all-to-all-done = f32[64,1,4224]{2,1,0:T(1,128)} async-done(((f32[64,1,4224]{2,1,0:T(1,128)}), f32[64,1,4224]{2,1,0:T(1,128)}, u32[]{:S(2)}, u32[]{:S(2)}) %all-to-all-start) | async-done | bytes 1081376 | tf_op jit(solution)/shard_map/all_to_all | solution.py:92
  122.4 3.1 %copy.58 = f32[64,1,4224]{0,2,1:T(8,128)S(1)} copy(f32[64,1,4224]{2,1,0:T(1,128)} %all-to-all-done) | data formatting | bytes 2162688 | tf_op jit(solution)/shard_map/all_to_all | solution.py:92
  126.3 0.7 fusion.26
  127.0 0.7 reduce_sum.62
  127.7 0.6 copy.63
  128.4 1.3 add_add_fusion
  129.7 0.8 copy.61
  130.5 0.8 copy.64
  131.7 0.6 fusion
  132.4 0.9 convolution_convert_fusion
  133.3 0.7 convert_element_type.119
  134.0 0.7 convert_element_type.120
  134.7 0.8 dynamic-slice_convert_fusion
  135.4 33.2 %reduce-scatter.2.cloned.1.call-done = bf16[16,256]{1,0:T(8,128)(2,1)} async-done(((bf16[16,2048]{1,0:T(8,128)(2,1)}), bf16[16,256]{1,0:T(8,128)(2,1)}) %reduce-scatter.2.cloned.1.call-update) | async-done | bytes 8208 | tf_op jit(solution)/shard_map/reduce_scatter | solution.py:137
  168.6 0.8 fusion.36
  169.4 15.6 %all-reduce = (f32[16]{0:T(128)S(1)}, f32[16]{0:T(128)S(1)}) all-reduce(f32[16]{0:T(128)S(1)} %get-tuple-element.7, f32[16]{0:T(128)S(1)} %get-tuple-element.6), channel_id=1, replica_groups=mesh['req'=64,'tp'=8] {'tp'}, use_global_device_ids=true, to_apply=%region_12.13 | all-reduce | flops 32 | bytes 256 | tf_op jit(solution)/shard_map/psum | solution.py:144
  185.0 1.4 add_convert_fusion
  (62 shorter events, 5.6 us)
Async XLA Ops:
  7.2 125.3 %copy-start = (bf16[256,2048]{1,0:T(8,128)(2,1)S(1)}, bf16[256,2048]{1,0:T(8,128)(2,1)}, u32[]{:S(2)}) copy-start(bf16[256,2048]{1,0:T(8,128)(2,1)} %param.22) | copy-start | bytes 3145732
  82.1 0.8 copy-start.5
  84.4 8.8 %copy-start.2 = (bf16[16,256]{1,0:T(8,128)(2,1)S(1)}, bf16[16,256]{1,0:T(8,128)(2,1)}, u32[]{:S(2)}) copy-start(bf16[16,256]{1,0:T(8,128)(2,1)} %param.13) | copy-start | bytes 24580
  84.4 8.8 %copy-start.3 = (bf16[16,2,256]{2,1,0:T(2,128)(2,1)S(1)}, bf16[16,2,256]{2,1,0:T(2,128)(2,1)}, u32[]{:S(2)}) copy-start(bf16[16,2,256]{2,1,0:T(2,128)(2,1)} %param.14) | copy-start | bytes 49156
  84.4 9.1 %copy-start.7 = (s32[16]{0:T(128)S(1)}, s32[16]{0:T(128)}, u32[]{:S(2)}) copy-start(s32[16]{0:T(128)} %param.16) | copy-start | bytes 196
  84.5 9.2 %copy-start.1 = (bf16[16,32,2,256]{3,2,1,0:T(2,128)(2,1)S(1)}, bf16[16,32,2,256]{3,2,1,0:T(2,128)(2,1)}, u32[]{:S(2)}) copy-start(bf16[16,32,2,256]{3,2,1,0:T(2,128)(2,1)} %param.15) | copy-start | bytes 1572868
  86.6 35.8 %all-to-all-start = ((f32[64,1,4224]{2,1,0:T(1,128)}), f32[64,1,4224]{2,1,0:T(1,128)}, u32[]{:S(2)}, u32[]{:S(2)}) async-start(f32[64,1,4224]{2,1,0:T(1,128)} %copy.57), calls=%async_computation | async-start | bytes 2162688 | tf_op jit(solution)/shard_map/all_to_all | solution.py:92
  93.0 75.6 %reduce-scatter.2.cloned.1.call-start = ((), (), s32[]{:S(2)}) async-start(), calls=%async_computation.2 | async-start | bytes 73728 | tf_op jit(solution)/shard_map/reduce_scatter | solution.py:137
  93.5 32.3 %copy-start.6 = (f32[16]{0:T(128)}, f32[16]{0:T(128)S(1)}, u32[]{:S(2)}) copy-start(f32[16]{0:T(128)S(1)} %convert_element_type.106) | copy-start | bytes 196
  169.4 17.0 %copy-start.4 = (bf16[16,256]{1,0:T(8,128)(2,1)}, bf16[16,256]{1,0:T(8,128)(2,1)S(1)}, u32[]{:S(2)}) copy-start(bf16[16,256]{1,0:T(8,128)(2,1)S(1)} %get-tuple-element.10) | copy-start | bytes 24580
Sparse Core Ops, SparseCore 0:
  133.5 35.0 reduce-scatter.1
where the time goes:
time: 194 us; the launch traced here: 193 us
  blocking collectives  71.6 us (37%)
  waiting for transfers between devices  59.4 us (31%)
  local copies, waits for them, and re-layouts  25.5 us (13%)
  between operations  14.3 us (7%)
  other arithmetic  11.6 us (6%)
  starting transfers between devices  6.56 us (3%)
  matrix products  4.23 us (2%)
    all_gather x1, blocking collectives, local(): everyone = lax.all_gather(queries, 'req', axis=0, tiled=True)  56 us
    reduce_scatter x1, waiting for transfers between devices, local(): lax.psum_scatter(partial_value.astype(jnp.bfloat16), 'tp', scatter_dimens...  33.2 us
    all_to_all x1, waiting for transfers between devices, local(): arrived = lax.all_to_all(packed, 'req', 0, 0, tiled=True)  26.2 us
    psum x1, blocking collectives, local(): lax.psum((jnp.sum(hidden_mine, -1), jnp.sum(hidden_mine * hidden_mine, -1...  15.6 us
    slice x1, local copies, waits for them, and re-layouts, local(): pool_cache[:, :, 1].reshape(page_count, PAGE, heads_here, HEAD)  10.7 us
    all_to_all x1, starting transfers between devices, local(): arrived = lax.all_to_all(packed, 'req', 0, 0, tiled=True)  6.34 us
    all_to_all x2, local copies, waits for them, and re-layouts, local(): arrived = lax.all_to_all(packed, 'req', 0, 0, tiled=True)  5.25 us
  transfers between devices with their start and end apart: 2, of which 2 were waited for; matrix products, arithmetic and copies ran while one was open for 3% of the time, Pallas kernels for 0%

commit v1 on v0

--- a/solution.py
+++ b/solution.py
@@ -44,7 +44,9 @@
     tail_slots = tail_cache.shape[1]
     n_req = lax.axis_size("req")
     assert group_count == n_req
-    everyone = lax.all_gather(queries, "req", axis=0, tiled=True)
+    everyone = jnp.concatenate(
+        lax.all_to_all(jnp.stack([queries] * lax.axis_size("req")), "req", 0, 0), axis=0
+    )
     by_group = everyone.reshape(group_count, row_count, heads_here, HEAD)
     safe_group = jnp.clip(page_group, 0, group_count - 1)
     page_queries = by_group[safe_group]

time: 194 us -> 158 us (0.81)
  blocking collectives: 71.6 us -> 15.6 us
  starting transfers between devices: 6.56 us -> 21.6 us
  waiting for transfers between devices: 59.4 us -> 62.3 us
  local copies, waits for them, and re-layouts: 25.5 us -> 28 us
    all_gather x1 -> x0, blocking collectives: 56 us -> none  [local(): everyone = lax.all_gather(queries, 'req', axis=0, tiled=True)]
    all_to_all x0 -> x1, starting transfers between devices: none -> 13.9 us  [local(): lax.all_to_all(jnp.stack([queries] * lax.axis_size('req')), 'req', 0, 0)]
    all_to_all x0 -> x1, waiting for transfers between devices: none -> 2.93 us  [local(): lax.all_to_all(jnp.stack([queries] * lax.axis_size('req')), 'req', 0, 0)]
  transfers between devices with their start and end apart: 2 -> 3, of which waited for: 2 -> 3; matrix products, arithmetic and copies ran while one was open for 3% -> 12% of each run, Pallas kernels for 0% -> 0%
where the time goes in v1:
time: 158 us
  waiting for transfers between devices  62.3 us (39%)
  local copies, waits for them, and re-layouts  28 us (18%)
  starting transfers between devices  21.6 us (14%)
  blocking collectives  15.6 us (10%)
  between operations  14.3 us (9%)
  other arithmetic  10.2 us (6%)
  matrix products  5.47 us (3%)
    reduce_scatter x1, waiting for transfers between devices, local(): lax.psum_scatter(partial_value.astype(jnp.bfloat16), 'tp', scatter_dimens...  33.2 us
    all_to_all x1, waiting for transfers between devices, local(): arrived = lax.all_to_all(packed, 'req', 0, 0, tiled=True)  26.2 us
    psum x1, blocking collectives, local(): lax.psum((jnp.sum(hidden_mine, -1), jnp.sum(hidden_mine * hidden_mine, -1...  15.6 us
    all_to_all x1, starting transfers between devices, local(): lax.all_to_all(jnp.stack([queries] * lax.axis_size('req')), 'req', 0, 0)  13.9 us
    slice x1, local copies, waits for them, and re-layouts, local(): pool_cache[:, :, 1].reshape(page_count, PAGE, heads_here, HEAD)  11.7 us
    all_to_all x1, starting transfers between devices, local(): arrived = lax.all_to_all(packed, 'req', 0, 0, tiled=True)  7.53 us
    all_to_all x2, local copies, waits for them, and re-layouts, local(): arrived = lax.all_to_all(packed, 'req', 0, 0, tiled=True)  5.25 us
  transfers between devices with their start and end apart: 3, of which 3 were waited for; matrix products, arithmetic and copies ran while one was open for 12% of the time, Pallas kernels for 0%

profile of v1, /device:TPU:2, one launch (start us, length us, event | category | flops | bytes accessed | tf_op | source)
XLA Modules:
  0.0 157.5 jit_solution(1046885522118408697)
XLA Ops:
  7.2 1.6 %stack.2 = bf16[64,16,256]{2,1,0:T(8,128)(2,1)} broadcast(bf16[16,256]{1,0:T(8,128)(2,1)} %param.13), dimensions={1,2} | broadcast | bytes 532480 | tf_op jit(solution)/shard_map/stack | solution.py:48
  8.8 13.9 %all-to-all-start = ((bf16[64,16,256]{2,1,0:T(8,128)(2,1)}), bf16[64,16,256]{2,1,0:T(8,128)(2,1)S(1)}, u32[]{:S(2)}, u32[]{:S(2)}) async-start(bf16[64,16,256]{2,1,0:T(8,128)(2,1)} %stack.2), calls=%async_computation | async-start | bytes 1048576 | tf_op jit(solution)/shard_map/all_to_all | solution.py:48
  22.7 0.7 compare_select_fusion
  23.4 0.7 broadcast_compare_fusion
  24.1 1.4 gather_fusion
  25.7 11.7 %slice_reduce_fusion = (bf16[32,64,256]{2,1,0:T(8,128)(2,1)S(1)}, bf16[32,64,256]{2,1,0:T(8,128)(2,1)}) fusion(bf16[32,64,2,256]{3,2,1,0:T(2,128)(2,1)} %param.17), kind=kLoop, calls=%fused_computation.7 | loop fusion | bytes 4194304 | tf_op jit(solution)/shard_map/slice | solution.py:54
  37.3 2.9 %all-to-all-done = bf16[64,16,256]{2,1,0:T(8,128)(2,1)S(1)} async-done(((bf16[64,16,256]{2,1,0:T(8,128)(2,1)}), bf16[64,16,256]{2,1,0:T(8,128)(2,1)S(1)}, u32[]{:S(2)}, u32[]{:S(2)}) %all-to-all-start) | async-done | bytes 524320 | tf_op jit(solution)/shard_map/all_to_all | solution.py:48
  40.4 0.6 gather_fusion.1
  41.0 2.0 %fusion.50 = (f32[32,16,2]{1,2,0:T(2,128)S(1)}, f32[32,16,2,64]{3,1,2,0:T(8,128)S(1)}) fusion(f32[32,2,64]{2,1,0:T(2,128)S(1)} %broadcast_multiply_fusion, bf16[32,16,2,128]{3,1,2,0:T(8,128)(2,1)S(1)} %gather_fusion.1, pred[32,64]{1,0:T(8,128)(4,1)S(1)} %get-tuple-element.24, bf16[32,64,256]{2,1,0:T(8,128)(2,1)} %get-tuple-element.3), kind=kOutput, calls=%fused_computation.96 | convolution fusion | flops 17038336 | bytes 1595392 | tf_op jit(solution)/shard_map/pqhd,pshd->pqhs/dot_general | solution.py:60
  43.3 0.6 gather_fusion.2
  43.9 0.4 fusion.12
  44.7 0.5 fusion.1
  47.6 2.1 %copy.57 = f32[64,1,4224]{2,1,0:T(1,128)} copy(f32[64,1,4224]{2,0,1:T(8,128)S(1)} %bitcast.92) | data formatting | bytes 2162688 | tf_op jit(solution)/shard_map/all_to_all | solution.py:94
  49.7 7.5 %all-to-all-start.1 = ((f32[64,1,4224]{2,1,0:T(1,128)}), f32[64,1,4224]{2,1,0:T(1,128)}, u32[]{:S(2)}, u32[]{:S(2)}) async-start(f32[64,1,4224]{2,1,0:T(1,128)} %copy.57), calls=%async_computation.1 | async-start | bytes 2162688 | tf_op jit(solution)/shard_map/all_to_all | solution.py:94
  58.0 2.2 %slice_reduce_fusion.2 = (bf16[16,32,256]{2,1,0:T(8,128)(2,1)S(1)}, bf16[16,32,256]{2,1,0:T(8,128)(2,1)S(1)}) fusion(bf16[16,32,2,256]{3,2,1,0:T(2,128)(2,1)S(1)} %copy-done.1), kind=kLoop, calls=%fused_computation.23 | loop fusion | bytes 1048576 | tf_op jit(solution)/shard_map/slice | solution.py:105
  60.5 26.2 %all-to-all-done.1 = f32[64,1,4224]{2,1,0:T(1,128)} async-done(((f32[64,1,4224]{2,1,0:T(1,128)}), f32[64,1,4224]{2,1,0:T(1,128)}, u32[]{:S(2)}, u32[]{:S(2)}) %all-to-all-start.1) | async-done | bytes 1081376 | tf_op jit(solution)/shard_map/all_to_all | solution.py:94
  86.7 3.1 %copy.58 = f32[64,1,4224]{0,2,1:T(8,128)S(1)} copy(f32[64,1,4224]{2,1,0:T(1,128)} %all-to-all-done.1) | data formatting | bytes 2162688 | tf_op jit(solution)/shard_map/all_to_all | solution.py:94
  90.6 0.7 fusion.26
  91.3 0.7 reduce_sum.62
  92.0 0.6 copy.63
  92.7 1.3 add_add_fusion
  94.0 0.8 copy.61
  94.8 0.8 copy.64
  96.0 0.6 fusion
  96.7 0.9 convolution_convert_fusion
  97.6 0.7 convert_element_type.119
  98.3 0.7 convert_element_type.120
  99.0 0.8 dynamic-slice_convert_fusion
  99.7 33.2 %reduce-scatter.2.cloned.1.call-done = bf16[16,256]{1,0:T(8,128)(2,1)} async-done(((bf16[16,2048]{1,0:T(8,128)(2,1)}), bf16[16,256]{1,0:T(8,128)(2,1)}) %reduce-scatter.2.cloned.1.call-update) | async-done | bytes 8208 | tf_op jit(solution)/shard_map/reduce_scatter | solution.py:139
  132.9 0.8 fusion.36
  133.7 15.6 %all-reduce = (f32[16]{0:T(128)S(1)}, f32[16]{0:T(128)S(1)}) all-reduce(f32[16]{0:T(128)S(1)} %get-tuple-element.7, f32[16]{0:T(128)S(1)} %get-tuple-element.6), channel_id=1, replica_groups=mesh['req'=64,'tp'=8] {'tp'}, use_global_device_ids=true, to_apply=%region_12.13 | all-reduce | flops 32 | bytes 256 | tf_op jit(solution)/shard_map/psum | solution.py:146
  149.3 1.4 add_convert_fusion
  (65 shorter events, 5.7 us)
Async XLA Ops:
  7.2 89.6 %copy-start = (bf16[256,2048]{1,0:T(8,128)(2,1)S(1)}, bf16[256,2048]{1,0:T(8,128)(2,1)}, u32[]{:S(2)}) copy-start(bf16[256,2048]{1,0:T(8,128)(2,1)} %param.22) | copy-start | bytes 3145732
  7.2 18.3 %copy-start.5 = (s32[32]{0:T(128)S(1)}, s32[32]{0:T(128)}, u32[]{:S(2)}) copy-start(s32[32]{0:T(128)} %param.18) | copy-start | bytes 388
  7.2 18.2 %copy-start.7 = (s32[32]{0:T(128)S(1)}, s32[32]{0:T(128)}, u32[]{:S(2)}) copy-start(s32[32]{0:T(128)} %param.19) | copy-start | bytes 388
  8.8 31.4 %all-to-all-start = ((bf16[64,16,256]{2,1,0:T(8,128)(2,1)}), bf16[64,16,256]{2,1,0:T(8,128)(2,1)S(1)}, u32[]{:S(2)}, u32[]{:S(2)}) async-start(bf16[64,16,256]{2,1,0:T(8,128)(2,1)} %stack.2), calls=%async_computation | async-start | bytes 1048576 | tf_op jit(solution)/shard_map/all_to_all | solution.py:48
  47.5 9.9 %copy-start.2 = (bf16[16,256]{1,0:T(8,128)(2,1)S(1)}, bf16[16,256]{1,0:T(8,128)(2,1)}, u32[]{:S(2)}) copy-start(bf16[16,256]{1,0:T(8,128)(2,1)} %param.13) | copy-start | bytes 24580
  47.5 10.0 %copy-start.3 = (bf16[16,2,256]{2,1,0:T(2,128)(2,1)S(1)}, bf16[16,2,256]{2,1,0:T(2,128)(2,1)}, u32[]{:S(2)}) copy-start(bf16[16,2,256]{2,1,0:T(2,128)(2,1)} %param.14) | copy-start | bytes 49156
  47.6 10.2 %copy-start.8 = (s32[16]{0:T(128)S(1)}, s32[16]{0:T(128)}, u32[]{:S(2)}) copy-start(s32[16]{0:T(128)} %param.16) | copy-start | bytes 196
  47.6 10.4 %copy-start.1 = (bf16[16,32,2,256]{3,2,1,0:T(2,128)(2,1)S(1)}, bf16[16,32,2,256]{3,2,1,0:T(2,128)(2,1)}, u32[]{:S(2)}) copy-start(bf16[16,32,2,256]{3,2,1,0:T(2,128)(2,1)} %param.15) | copy-start | bytes 1572868
  49.7 37.0 %all-to-all-start.1 = ((f32[64,1,4224]{2,1,0:T(1,128)}), f32[64,1,4224]{2,1,0:T(1,128)}, u32[]{:S(2)}, u32[]{:S(2)}) async-start(f32[64,1,4224]{2,1,0:T(1,128)} %copy.57), calls=%async_computation.1 | async-start | bytes 2162688 | tf_op jit(solution)/shard_map/all_to_all | solution.py:94
  57.3 75.6 %reduce-scatter.2.cloned.1.call-start = ((), (), s32[]{:S(2)}) async-start(), calls=%async_computation.3 | async-start | bytes 73728 | tf_op jit(solution)/shard_map/reduce_scatter | solution.py:139
  57.8 32.3 %copy-start.6 = (f32[16]{0:T(128)}, f32[16]{0:T(128)S(1)}, u32[]{:S(2)}) copy-start(f32[16]{0:T(128)S(1)} %convert_element_type.106) | copy-start | bytes 196
  133.7 17.0 %copy-start.4 = (bf16[16,256]{1,0:T(8,128)(2,1)}, bf16[16,256]{1,0:T(8,128)(2,1)S(1)}, u32[]{:S(2)}) copy-start(bf16[16,256]{1,0:T(8,128)(2,1)S(1)} %get-tuple-element.10) | copy-start | bytes 24580
Sparse Core Ops, SparseCore 0:
  97.8 35.0 reduce-scatter.1
